TPU v7x, 512 devices: a whole 4x8x8 slice. The times are simulated.
512 devices in a mesh: blk: 32 (over y, z_hi), kv: 16 (over z_lo, x, core).
Axes of the slice: x: 4, y: 8, z: 8 (z_hi: 4, z_lo: 2; z = z_hi * 2 + z_lo), core: 2. Of those that a mesh axis runs over, the one named last changes fastest.
Arguments:
- cache_entries: bfloat16 [65536, 8, 256], P(('kv', 'blk'))
- recompute_input: bfloat16 [4096, 4096], P('kv', 'blk'), may hold values from -6 to 6
- norm_gain: bfloat16 [4096], replicated, may hold values from 0.099609375 to 1.8984375
- w_query: bfloat16 [4096, 4096], P(None, 'blk'), may hold values from -0.25 to 0.25
- w_keyval: bfloat16 [4096, 2048], P('blk'), may hold values from -0.09375 to 0.09375
- w_out: bfloat16 [4096, 4096], P('blk'), may hold values from -0.09375 to 0.09375
- rotate_offsets: int32 [64], replicated, may hold values from 0 to 65535
- span_order: int32 [64], replicated, may hold values from 0 to 63, as said below
- tenant_of_span: int32 [64], replicated, may hold values from 0 to 3, never falling along the last dimension, each value on 1 to 32 neighbouring positions
- recompute_pos: int32 [4096], replicated, may hold values from 0 to 4095, as said below
- recompute_count: int32 [16], replicated, may hold values from 1 to 256, as said below
Outputs:
- attention_out: bfloat16 [4096, 4096], P('kv', 'blk')
Inputs may be any that keep to these rules, and one draw needn't show every extreme that they name: `span_order`: each aligned block of 4 entries is a permutation of the block slots of that same block. `tenant_of_span`: tenants never fall along the block slots; there are 4 tenants, one of exactly 32 blocks. `recompute_pos`: the 256 entries of each shard are distinct. `recompute_count`: at least one shard has all 256 slots live.
All inputs are finite; a program needn't handle non-finite values.
Results may differ from a plain program's by a relative error of at most 0.035.
Values may be sent and summed in bfloat16 or wider, within the bound.
No kernel may reach another device: no remote copies, remote signals or barrier semaphores. Data moves between devices by JAX's collectives and lax.ppermute only.
A program may use at most 64 MiB of HBM per device.

v0:
```python
import math
import jax
import jax.numpy as jnp
import numpy as np
from jax import lax
from jax.sharding import PartitionSpec as P

QH = 32
KVH = 8
HEAD_DIM = 128
WINDOW = 4096
SPAN = 1024
NEG_FILL = -1e30
ROPE_BASE = 10000.0
NORM_EPS = 1e-05


def shifted(shard, axis, by):
    devices = lax.axis_size(axis)
    pairs = [(i, i + by) for i in range(devices) if 0 <= i + by < devices]
    return lax.ppermute(shard, axis, pairs)


def rotate_half(values, positions):
    half = values.shape[-1] // 2
    inverse = ROPE_BASE ** (-(jnp.arange(half, dtype=jnp.float32) * 2.0 / values.shape[-1]))
    angles = positions.astype(jnp.float32)[:, None] * inverse[None, :]
    shape = (positions.shape[0],) + (1,) * (values.ndim - 2) + (half,)
    cosine = jnp.cos(angles).reshape(shape)
    sine = jnp.sin(angles).reshape(shape)
    first = values[..., :half]
    second = values[..., half:]
    return jnp.concatenate(
        [first * cosine - second * sine, second * cosine + first * sine], axis=-1
    )


def tenant_lookup(positions, tenant_of_span):
    span_ids = positions // SPAN
    table_index = jnp.arange(tenant_of_span.shape[0], dtype=jnp.int32)
    match = span_ids[:, None] == table_index[None, :]
    return jnp.sum(jnp.where(match, tenant_of_span[None, :], 0), axis=1)


def attend_part(queries, query_pos, query_tenant, keys, values, key_pos, key_tenant):
    scale = 1.0 / math.sqrt(keys.shape[-1])
    scores = jnp.einsum("cgh,sh->gcs", queries, keys, preferred_element_type=jnp.float32) * scale
    gap = query_pos[:, None] - key_pos[None, :]
    allowed = (
        (query_tenant[:, None] == key_tenant[None, :])
        & (gap >= 0)
        & (gap < WINDOW)
        & (key_pos[None, :] >= 0)
    )
    masked = jnp.where(allowed[None], scores, NEG_FILL)
    row_max = jnp.max(masked, axis=2)
    weights = jnp.where(allowed[None], jnp.exp(masked - row_max[..., None]), 0.0)
    totals = jnp.sum(weights, axis=2)
    summed = jnp.einsum(
        "gcs,sh->gch", weights.astype(jnp.bfloat16), values, preferred_element_type=jnp.float32
    )
    return (row_max, totals, summed)


def combine_parts(first, second):
    top = jnp.maximum(first[0], second[0])
    scale_one = jnp.exp(first[0] - top)
    scale_two = jnp.exp(second[0] - top)
    totals = first[1] * scale_one + second[1] * scale_two
    summed = first[2] * scale_one[..., None] + second[2] * scale_two[..., None]
    return summed / totals[..., None]


def local(
    cache_entries,
    recompute_input,
    norm_gain,
    w_query,
    w_keyval,
    w_out,
    rotate_offsets,
    span_order,
    tenant_of_span,
    recompute_pos,
    recompute_count,
):
    blk_count = lax.axis_size("blk")
    kv_index = lax.axis_index("kv")
    blk_index = lax.axis_index("blk")
    block_rows = cache_entries.shape[0]
    shard_len = block_rows * blk_count
    slots = recompute_input.shape[0]
    own_cols = recompute_input.shape[1]
    width = norm_gain.shape[0]
    local_heads = w_query.shape[1] // HEAD_DIM
    spans_here = shard_len // SPAN
    own_group = blk_index * local_heads // (QH // KVH)
    targets = np.arange(blk_count) * local_heads // (QH // KVH)
    wide = lax.all_gather(recompute_input, "blk", axis=1, tiled=True).astype(jnp.float32)
    gains = norm_gain.astype(jnp.float32)
    scaled = (wide * gains[None, :]).astype(jnp.bfloat16)
    query_acc = jnp.dot(scaled, w_query, preferred_element_type=jnp.float32)
    square_acc = jnp.sum(wide * wide, axis=1)
    own_gain = lax.dynamic_slice_in_dim(norm_gain, blk_index * own_cols, own_cols, 0).astype(
        jnp.float32
    )
    own_scaled = (recompute_input.astype(jnp.float32) * own_gain[None, :]).astype(jnp.bfloat16)
    pair_term = jnp.dot(own_scaled, w_keyval, preferred_element_type=jnp.float32)
    pair_sum = lax.psum(pair_term.astype(jnp.bfloat16), "blk").astype(jnp.float32)
    inv_rms = lax.rsqrt(square_acc / width + NORM_EPS)
    pair_heads = (pair_sum * inv_rms[:, None]).reshape(slots, KVH, 2 * HEAD_DIM)
    own_pair = lax.dynamic_index_in_dim(pair_heads, own_group, 1, keepdims=False)
    own_pos = lax.dynamic_slice_in_dim(recompute_pos, kv_index * slots, slots, 0)
    own_count = lax.dynamic_index_in_dim(recompute_count, kv_index, 0, keepdims=False)
    live = jnp.arange(slots, dtype=jnp.int32) < own_count
    query_pos = kv_index * shard_len + own_pos
    fresh_keys = rotate_half(own_pair[:, :HEAD_DIM], query_pos).astype(jnp.bfloat16)
    fresh_values = own_pair[:, HEAD_DIM:].astype(jnp.bfloat16)
    queries = rotate_half(
        (query_acc * inv_rms[:, None]).reshape(slots, local_heads, HEAD_DIM), query_pos
    ).astype(jnp.bfloat16)
    arrived = lax.all_to_all(
        jnp.take(cache_entries, targets, axis=1), "blk", split_axis=1, concat_axis=0, tiled=True
    )
    stored = arrived.reshape(shard_len, 2 * HEAD_DIM)
    offsets_here = lax.dynamic_slice_in_dim(rotate_offsets, kv_index * spans_here, spans_here, 0)
    row_shifts = jnp.repeat(offsets_here, SPAN, total_repeat_length=shard_len)
    turned_rows = rotate_half(stored[:, :HEAD_DIM].astype(jnp.float32), row_shifts).astype(
        jnp.bfloat16
    )
    stored = jnp.concatenate([turned_rows, stored[:, HEAD_DIM:]], axis=-1)
    local_order = (
        lax.dynamic_slice_in_dim(span_order, kv_index * spans_here, spans_here, 0)
        - kv_index * spans_here
    )
    ordered = jnp.take(stored.reshape(spans_here, SPAN, 2 * HEAD_DIM), local_order, axis=0).reshape(
        shard_len, 2 * HEAD_DIM
    )
    place = jnp.where(live, own_pos, shard_len)
    merged = ordered.at[place].set(jnp.concatenate([fresh_keys, fresh_values], axis=1), mode="drop")
    key_pos = kv_index * shard_len + jnp.arange(shard_len, dtype=jnp.int32)
    key_tenant = tenant_lookup(key_pos, tenant_of_span)
    query_tenant = tenant_lookup(query_pos, tenant_of_span)
    own_part = attend_part(
        queries,
        query_pos,
        query_tenant,
        merged[:, :HEAD_DIM],
        merged[:, HEAD_DIM:],
        key_pos,
        key_tenant,
    )
    prior = shifted(merged, "kv", 1)
    prior_pos = key_pos - shard_len
    prior_part = attend_part(
        queries,
        query_pos,
        query_tenant,
        prior[:, :HEAD_DIM],
        prior[:, HEAD_DIM:],
        prior_pos,
        tenant_lookup(prior_pos, tenant_of_span),
    )
    heads_out = combine_parts(own_part, prior_part).astype(jnp.bfloat16)
    out_rows = w_out.reshape(local_heads, HEAD_DIM, width)
    term = jnp.einsum("gch,ghd->cd", heads_out, out_rows, preferred_element_type=jnp.float32)
    summed_out = lax.psum_scatter(
        term.astype(jnp.bfloat16), "blk", scatter_dimension=1, tiled=True
    ).astype(jnp.float32)
    return jnp.where(live[:, None], summed_out, 0.0).astype(jnp.bfloat16)


def solution(mesh):
    placed = (
        P(("kv", "blk"), None, None),
        P("kv", "blk"),
        P(),
        P(None, "blk"),
        P("blk", None),
        P("blk", None),
        P(),
        P(),
        P(),
        P(),
        P(),
    )
    return jax.shard_map(
        local, mesh=mesh, in_specs=placed, out_specs=P("kv", "blk"), check_vma=False
    )
```

profile of v0, /device:TPU:2, one launch (start us, length us, event | category | flops | bytes accessed | tf_op | source)
XLA Modules:
  0.0 771.2 jit_solution(2034141246028215434)
XLA Ops:
  6.5 0.0 copy-start
  6.5 0.0 all-gather.2.cloned.1.call-start
  6.5 0.7 all-gather.2.cloned.1.call-update
  7.3 0.7 pad_clamp_fusion.1
  7.9 6.6 gather_fusion
  14.5 0.0 copy-start.4
  14.5 0.0 copy-start.3
  14.5 2.5 copy.21
  17.0 0.0 copy-start.6
  17.0 0.0 copy-start.7
  17.0 16.1 %all-to-all-start = ((bf16[128,32,256]{2,0,1:T(8,128)(2,1)}), bf16[128,32,256]{2,0,1:T(8,128)(2,1)S(1)}, u32[]{:S(2)}, u32[]{:S(2)}) async-start(bf16[128,32,256]{2,0,1:T(8,128)(2,1)} %copy.21), calls=%async_computation | async-start | bytes 4194304 | tf_op jit(solution)/shard_map/all_to_all | solution.py:122
  33.1 0.0 all-reduce.2.cloned.1.call-start
  33.2 0.0 copy-done.4
  33.2 0.1 dynamic-slice_convert_fusion
  33.3 0.0 copy-done.3
  33.3 2.4 convolution_convert_fusion.1
  35.7 0.0 all-reduce.2.cloned.1.call-update
  35.7 0.2 reduce-scatter.4.cloned.1.call-start
  36.0 0.0 copy-done.11
  36.0 0.6 dynamic_slice.20
  36.6 0.1 compare_and_fusion
  36.7 0.1 broadcast_bitcast_fusion
  36.7 1.4 and_select_fusion
  38.2 0.1 dynamic_slice.23
  38.3 0.7 fusion.108
  38.9 0.0 copy-done.5
  39.0 2.6 select_convert_fusion.1
  41.5 101.7 %all-gather.2.cloned.1.call-done = bf16[256,4096]{1,0:T(8,128)(2,1)} async-done(((bf16[256,128]{1,0:T(8,128)(2,1)}), bf16[256,4096]{1,0:T(8,128)(2,1)}) %all-gather.2.cloned.1.call-update) | async-done | bytes 2097168 | tf_op jit(solution)/shard_map/all_gather | solution.py:99
  143.3 2.1 fusion.4
  145.4 315.9 %all-reduce.2.cloned.1.call-done = bf16[256,2048]{1,0:T(8,128)(2,1)} async-done(((bf16[256,2048]{1,0:T(8,128)(2,1)}), bf16[256,2048]{1,0:T(8,128)(2,1)}) %all-reduce.2.cloned.1.call-update) | async-done | bytes 1048592 | tf_op jit(solution)/shard_map/psum | solution.py:109
  461.3 2.8 convert_multiply_fusion.2
  464.0 2.9 copy.27
  466.9 1.0 dynamic-slice_bitcast_fusion
  467.9 0.3 fusion.78
  468.3 0.1 copy.26
  468.4 0.0 all-to-all-done
  468.4 1.5 fusion.107
  469.8 1.5 copy.30
  471.3 0.2 convert_element_type.65
  471.5 5.4 fusion.57
  476.9 0.5 copy.23
  477.4 1.5 copy.24
  478.9 3.5 pad_maximum_fusion
  482.4 2.3 gather_fusion.1
  484.7 0.0 copy-start.8
  484.7 1.9 bitcast_select_fusion
  486.6 4.8 scatter_fusion
  491.4 2.1 collective-permute-start
  493.6 0.1 select_reduce_fusion.2
  493.7 0.4 select_reduce_fusion
  494.1 2.7 fusion.36
  496.7 0.3 fusion.85
  497.1 3.5 fusion.109
  500.6 18.3 %collective-permute-done = bf16[4096,256]{1,0:T(8,128)(2,1)S(1)} collective-permute-done((bf16[4096,256]{1,0:T(8,128)(2,1)}, bf16[4096,256]{1,0:T(8,128)(2,1)S(1)}, u32[]{:S(2)}, u32[]{:S(2)}) %collective-permute-start) | collective-permute-done | bytes 2097184 | tf_op jit(solution)/shard_map/ppermute | solution.py:21
  518.9 1.8 fusion.110
  520.7 5.8 fusion.12
  526.5 3.0 fusion.39
  529.5 5.8 convolution_convert_fusion
  535.3 2.5 copy.28
  537.8 0.0 reduce-scatter.4.cloned.1.call-update
  537.8 0.7 iota_compare_fusion.3
  538.5 224.5 %reduce-scatter.4.cloned.1.call-done = bf16[128,256]{1,0:T(8,128)(2,1)} async-done(((bf16[4096,256]{1,0:T(8,128)(2,1)}), bf16[128,256]{1,0:T(8,128)(2,1)}) %reduce-scatter.4.cloned.1.call-update) | async-done | bytes 65552
  763.0 0.9 copy.29
  763.9 0.7 select_convert_fusion
  (28 shorter events, 0.1 us)
Async XLA Ops:
  6.5 523.0 %copy-start = (bf16[128,4096]{1,0:T(8,128)(2,1)S(1)}, bf16[128,4096]{1,0:T(8,128)(2,1)}, u32[]{:S(2)}) copy-start(bf16[128,4096]{1,0:T(8,128)(2,1)} %param.19) | copy-start | bytes 3145732
  6.5 136.7 %all-gather.2.cloned.1.call-start = ((), (), s32[]{:S(2)}) async-start(), calls=%async_computation.3 | async-start | bytes 2162688 | tf_op jit(solution)/shard_map/all_gather | solution.py:99
  14.5 18.7 %copy-start.4 = (bf16[4096]{0:T(1024)(128)(2,1)S(1)}, bf16[4096]{0:T(1024)(128)(2,1)}, u32[]{:S(2)}) copy-start(bf16[4096]{0:T(1024)(128)(2,1)} %param.16) | copy-start | bytes 24580
  14.5 18.8 %copy-start.3 = (bf16[256,128]{1,0:T(8,128)(2,1)S(1)}, bf16[256,128]{1,0:T(8,128)(2,1)}, u32[]{:S(2)}) copy-start(bf16[256,128]{1,0:T(8,128)(2,1)} %param.15) | copy-start | bytes 196612
  17.0 19.0 %copy-start.11 = (s32[16]{0:T(128)S(1)}, s32[16]{0:T(128)}, u32[]{:S(2)}) copy-start(s32[16]{0:T(128)} %param.24) | copy-start | bytes 196
  17.0 19.6 %copy-start.9 = (s32[64]{0:T(128)S(1)}, s32[64]{0:T(128)}, u32[]{:S(2)}) copy-start(s32[64]{0:T(128)} %param.21) | copy-start | bytes 772
  17.0 21.2 %copy-start.12 = (s32[64]{0:T(128)S(1)}, s32[64]{0:T(128)}, u32[]{:S(2)}) copy-start(s32[64]{0:T(128)} %param.20) | copy-start | bytes 772
  17.0 21.9 %copy-start.5 = (pred[4096]{0:T(1024)(128)(4,1)S(1)}, pred[4096]{0:T(1024)(128)(4,1)}, u32[]{:S(2)}) copy-start(pred[4096]{0:T(1024)(128)(4,1)} %constant.245) | copy-start | bytes 12292
  17.0 21.9 %copy-start.6 = (pred[4096]{0:T(1024)(128)(4,1)S(1)}, pred[4096]{0:T(1024)(128)(4,1)}, u32[]{:S(2)}) copy-start(pred[4096]{0:T(1024)(128)(4,1)} %constant.244) | copy-start | bytes 12292
  17.0 21.9 %copy-start.7 = (pred[4096]{0:T(1024)(128)(4,1)S(1)}, pred[4096]{0:T(1024)(128)(4,1)}, u32[]{:S(2)}) copy-start(pred[4096]{0:T(1024)(128)(4,1)} %constant.243) | copy-start | bytes 12292
  17.0 451.3 %all-to-all-start = ((bf16[128,32,256]{2,0,1:T(8,128)(2,1)}), bf16[128,32,256]{2,0,1:T(8,128)(2,1)S(1)}, u32[]{:S(2)}, u32[]{:S(2)}) async-start(bf16[128,32,256]{2,0,1:T(8,128)(2,1)} %copy.21), calls=%async_computation | async-start | bytes 4194304 | tf_op jit(solution)/shard_map/all_to_all | solution.py:122
  33.1 428.1 %all-reduce.2.cloned.1.call-start = ((), (), s32[]{:S(2)}) async-start(), calls=%async_computation.2 | async-start | bytes 2097152 | tf_op jit(solution)/shard_map/psum | solution.py:109
  35.7 727.3 %reduce-scatter.4.cloned.1.call-start = ((), (), s32[]{:S(2)}) async-start(), calls=%async_computation.4 | async-start | bytes 2162688
  484.7 8.9 %copy-start.8 = (s32[64]{0:T(128)S(1)}, s32[64]{0:T(128)}, u32[]{:S(2)}) copy-start(s32[64]{0:T(128)} %param.22) | copy-start | bytes 772
  491.4 27.6 %collective-permute-start = (bf16[4096,256]{1,0:T(8,128)(2,1)}, bf16[4096,256]{1,0:T(8,128)(2,1)S(1)}, u32[]{:S(2)}, u32[]{:S(2)}) collective-permute-start(bf16[4096,256]{1,0:T(8,128)(2,1)} %scatter_fusion), channel_id=1, source_target_pairs={{0,1},{1,2},{2,3},{3,4},{4,5},{5,6},{6,7},{7,8},{8,9},{9,10},{10,1... | collective-permute-start | bytes 6291464 | tf_op jit(solution)/shard_map/ppermute | solution.py:21
  518.9 1.8 copy-start.10
  520.7 5.8 copy-start.2
  520.7 5.8 copy-start.1
Sparse Core Ops, SparseCore 0:
  10.4 132.8 all-gather.1
  146.2 315.0 all-reduce.1
  538.0 224.9 reduce-scatter.3
where the time goes:
time: 772 us; the launch traced here: 771 us
  waiting for transfers between devices  661 us (86%)
  local copies, waits for them, and re-layouts  29.9 us (4%)
  other arithmetic  29 us (4%)
  matrix products  19.2 us (2%)
  starting transfers between devices  18.5 us (2%)
  between operations  13.5 us (2%)
    psum x1, waiting for transfers between devices, local(): lax.psum(pair_term.astype(jnp.bfloat16), 'blk').astype(jnp.float32)  316 us
    unnamed x4, waiting for transfers between devices  225 us
    all_gather x1, waiting for transfers between devices, local(): lax.all_gather(recompute_input, 'blk', axis=1, tiled=True)  102 us
    ppermute x1, waiting for transfers between devices, shifted(): return lax.ppermute(shard, axis, pairs)  18.3 us
    all_to_all x1, starting transfers between devices, local(): lax.all_to_all(jnp.take(cache_entries, targets, axis=1), 'blk', split_axi...  16.1 us
  transfers between devices with their start and end apart: 5, of which 4 were waited for; matrix products, arithmetic and copies ran while one was open for 4% of the time, Pallas kernels for 0%

commit v1 on v0

--- a/solution.py
+++ b/solution.py
@@ -13,6 +13,12 @@
 NEG_FILL = -1e30
 ROPE_BASE = 10000.0
 NORM_EPS = 1e-05
+
+
+def gather_and_add(x, axis):
+    blocks = lax.all_gather(x, axis, axis=0, tiled=False)
+    total = blocks.sum(axis=0)
+    return total
 
 
 def shifted(shard, axis, by):
@@ -106,7 +112,7 @@
     )
     own_scaled = (recompute_input.astype(jnp.float32) * own_gain[None, :]).astype(jnp.bfloat16)
     pair_term = jnp.dot(own_scaled, w_keyval, preferred_element_type=jnp.float32)
-    pair_sum = lax.psum(pair_term.astype(jnp.bfloat16), "blk").astype(jnp.float32)
+    pair_sum = gather_and_add(pair_term.astype(jnp.bfloat16), "blk").astype(jnp.float32)
     inv_rms = lax.rsqrt(square_acc / width + NORM_EPS)
     pair_heads = (pair_sum * inv_rms[:, None]).reshape(slots, KVH, 2 * HEAD_DIM)
     own_pair = lax.dynamic_index_in_dim(pair_heads, own_group, 1, keepdims=False)

time: 772 us -> 830 us (1.075)
  waiting for transfers between devices: 661 us -> 702 us
  other arithmetic: 29 us -> 49.8 us
    all_gather x0 -> x1, waiting for transfers between devices: none -> 380 us  [gather_and_add(): blocks = lax.all_gather(x, axis, axis=0, tiled=False)]
    psum x1 -> x0, waiting for transfers between devices: 316 us -> none  [local(): lax.psum(pair_term.astype(jnp.bfloat16), 'blk').astype(jnp.float32)]
    all_gather x1, waiting for transfers between devices: 102 us -> 32.2 us  [local(): lax.all_gather(recompute_input, 'blk', axis=1, tiled=True)]
    all_to_all x1, waiting for transfers between devices: 0.01 us -> 47.1 us  [local(): lax.all_to_all(jnp.take(cache_entries, targets, axis=1), 'blk', split_axi...]
    reduce_sum x0 -> x1, other arithmetic: none -> 11.5 us  [gather_and_add(): total = blocks.sum(axis=0)]
  transfers between devices with their start and end apart: 5 -> 5, of which waited for: 4 -> 5; matrix products, arithmetic and copies ran while one was open for 4% -> 6% of each run, Pallas kernels for 0% -> 0%
where the time goes in v1:
time: 830 us; the launch traced here: 829 us
  waiting for transfers between devices  702 us (85%)
  other arithmetic  49.8 us (6%)
  local copies, waits for them, and re-layouts  26.1 us (3%)
  matrix products  18.7 us (2%)
  starting transfers between devices  18.3 us (2%)
  between operations  13.4 us (2%)
    all_gather x1, waiting for transfers between devices, gather_and_add(): blocks = lax.all_gather(x, axis, axis=0, tiled=False)  380 us
    unnamed x4, waiting for transfers between devices  226 us
    all_to_all x1, waiting for transfers between devices, local(): lax.all_to_all(jnp.take(cache_entries, targets, axis=1), 'blk', split_axi...  47.1 us
    all_gather x1, waiting for transfers between devices, local(): lax.all_gather(recompute_input, 'blk', axis=1, tiled=True)  32.2 us
    ppermute x1, waiting for transfers between devices, shifted(): return lax.ppermute(shard, axis, pairs)  16.9 us
  transfers between devices with their start and end apart: 5, of which 5 were waited for; matrix products, arithmetic and copies ran while one was open for 6% of the time, Pallas kernels for 0%

profile of v1, /device:TPU:2, one launch (start us, length us, event | category | flops | bytes accessed | tf_op | source)
XLA Modules:
  0.0 828.7 jit_solution(376086353432289511)
XLA Ops:
  6.5 0.0 copy-start
  6.5 0.0 all-gather.4.cloned.1.call-start
  6.5 0.7 all-gather.4.cloned.1.call-update
  7.3 0.0 all-gather.6.cloned.1.call-start
  7.3 0.8 dynamic-slice_convert_fusion
  8.1 2.5 convolution_convert_fusion.1
  10.6 0.0 all-gather.6.cloned.1.call-update
  10.6 0.7 pad_clamp_fusion.1
  11.3 0.0 copy-done.1
  11.3 7.8 gather_fusion
  19.1 0.0 copy-start.6
  19.1 0.0 copy-start.7
  19.1 4.2 copy.23
  23.3 16.0 %all-to-all-start = ((bf16[128,32,256]{2,0,1:T(8,128)(2,1)}), bf16[128,32,256]{2,0,1:T(8,128)(2,1)S(1)}, u32[]{:S(2)}, u32[]{:S(2)}) async-start(bf16[128,32,256]{2,0,1:T(8,128)(2,1)} %copy.23), calls=%async_computation | async-start | bytes 4194304 | tf_op jit(solution)/shard_map/all_to_all | solution.py:128
  39.3 0.2 reduce-scatter.4.cloned.1.call-start
  39.6 0.6 dynamic_slice.20
  40.2 2.0 and_select_fusion
  42.1 0.0 copy-done.11
  42.1 0.1 dynamic_slice.23
  42.2 0.1 compare_and_fusion
  42.3 0.1 broadcast_bitcast_fusion
  42.4 0.7 fusion.114
  43.1 2.6 select_convert_fusion.1
  45.7 47.1 %all-to-all-done = bf16[128,32,256]{2,0,1:T(8,128)(2,1)S(1)} async-done(((bf16[128,32,256]{2,0,1:T(8,128)(2,1)}), bf16[128,32,256]{2,0,1:T(8,128)(2,1)S(1)}, u32[]{:S(2)}, u32[]{:S(2)}) %all-to-all-start) | async-done | bytes 2097184 | tf_op jit(solution)/shard_map/all_to_all | solution.py:128
  92.8 1.4 fusion.113
  94.3 1.5 copy.37
  95.7 0.2 convert_element_type.71
  96.0 5.3 fusion.57
  101.3 0.5 copy.25
  101.8 1.5 copy.26
  103.3 3.6 pad_maximum_fusion
  106.9 2.3 gather_fusion.1
  109.2 32.2 %all-gather.4.cloned.1.call-done = bf16[256,4096]{1,0:T(8,128)(2,1)} async-done(((bf16[256,128]{1,0:T(8,128)(2,1)}), bf16[256,4096]{1,0:T(8,128)(2,1)}) %all-gather.4.cloned.1.call-update) | async-done | bytes 2097168 | tf_op jit(solution)/shard_map/all_gather | solution.py:105
  141.4 2.1 fusion.4
  143.5 1.9 bitcast_select_fusion
  145.4 380.2 %all-gather.6.cloned.1.call-done = bf16[8192,2048]{1,0:T(8,128)(2,1)} async-done(((bf16[256,2048]{1,0:T(8,128)(2,1)}), bf16[8192,2048]{1,0:T(8,128)(2,1)}) %all-gather.6.cloned.1.call-update) | async-done | bytes 33554448 | tf_op jit(solution)/shard_map/all_gather | solution.py:19
  525.6 11.5 %reduce_sum.68 = bf16[256,2048]{1,0:T(8,128)(2,1)S(1)} reduce(bf16[32,256,2048]{2,1,0:T(8,128)(2,1)} %bitcast.67, bf16[]{:T(256)} %constant.220.clone.1), dimensions={0}, to_apply=%region_2.3 | reduce | flops 16252928 | bytes 34603008 | tf_op jit(solution)/shard_map/reduce_sum | solution.py:20
  537.0 1.6 copy.27
  538.7 1.8 fusion.120
  540.5 1.0 dynamic-slice_multiply_fusion
  541.4 0.1 copy.28
  541.6 1.2 fusion.84
  542.8 0.1 copy.31
  542.9 0.1 copy.32
  543.0 5.1 scatter_custom_fusion
  548.1 2.1 collective-permute-start
  550.2 0.7 convert_element_type.81
  551.0 0.8 select_reduce_fusion.2
  551.8 1.0 select_reduce_fusion
  552.8 0.0 copy-done.4
  552.8 2.0 fusion.36
  554.9 0.3 fusion.91
  555.2 3.5 fusion.115
  558.8 16.9 %collective-permute-done = bf16[4096,256]{1,0:T(8,128)(2,1)S(1)} collective-permute-done((bf16[4096,256]{1,0:T(8,128)(2,1)}, bf16[4096,256]{1,0:T(8,128)(2,1)S(1)}, u32[]{:S(2)}, u32[]{:S(2)}) %collective-permute-start) | collective-permute-done | bytes 2097184 | tf_op jit(solution)/shard_map/ppermute | solution.py:27
  575.6 1.8 fusion.116
  577.4 5.8 fusion.12
  583.3 3.0 fusion.39
  586.3 5.8 convolution_convert_fusion
  592.1 2.5 copy.35
  594.6 0.0 reduce-scatter.4.cloned.1.call-update
  594.6 0.6 iota_compare_fusion.3
  595.2 225.2 %reduce-scatter.4.cloned.1.call-done = bf16[128,256]{1,0:T(8,128)(2,1)} async-done(((bf16[4096,256]{1,0:T(8,128)(2,1)}), bf16[128,256]{1,0:T(8,128)(2,1)}) %reduce-scatter.4.cloned.1.call-update) | async-done | bytes 65552
  820.5 0.9 copy.36
  821.4 0.7 select_convert_fusion
  (28 shorter events, 0.1 us)
Async XLA Ops:
  6.5 579.8 %copy-start = (bf16[128,4096]{1,0:T(8,128)(2,1)S(1)}, bf16[128,4096]{1,0:T(8,128)(2,1)}, u32[]{:S(2)}) copy-start(bf16[128,4096]{1,0:T(8,128)(2,1)} %param.19) | copy-start | bytes 3145732
  6.5 4.7 copy-start.1
  6.5 134.9 %all-gather.4.cloned.1.call-start = ((), (), s32[]{:S(2)}) async-start(), calls=%async_computation.2 | async-start | bytes 2162688 | tf_op jit(solution)/shard_map/all_gather | solution.py:105
  7.3 518.3 %all-gather.6.cloned.1.call-start = ((), (), s32[]{:S(2)}) async-start(), calls=%async_computation.3 | async-start | bytes 34603008 | tf_op jit(solution)/shard_map/all_gather | solution.py:19
  19.1 20.5 %copy-start.10 = (s32[16]{0:T(128)S(1)}, s32[16]{0:T(128)}, u32[]{:S(2)}) copy-start(s32[16]{0:T(128)} %param.24) | copy-start | bytes 196
  19.1 23.0 %copy-start.11 = (s32[64]{0:T(128)S(1)}, s32[64]{0:T(128)}, u32[]{:S(2)}) copy-start(s32[64]{0:T(128)} %param.20) | copy-start | bytes 772
  19.1 23.1 %copy-start.8 = (s32[64]{0:T(128)S(1)}, s32[64]{0:T(128)}, u32[]{:S(2)}) copy-start(s32[64]{0:T(128)} %param.21) | copy-start | bytes 772
  19.1 24.0 %copy-start.5 = (pred[4096]{0:T(1024)(128)(4,1)S(1)}, pred[4096]{0:T(1024)(128)(4,1)}, u32[]{:S(2)}) copy-start(pred[4096]{0:T(1024)(128)(4,1)} %constant.247) | copy-start | bytes 12292
  19.1 24.0 %copy-start.6 = (pred[4096]{0:T(1024)(128)(4,1)S(1)}, pred[4096]{0:T(1024)(128)(4,1)}, u32[]{:S(2)}) copy-start(pred[4096]{0:T(1024)(128)(4,1)} %constant.246) | copy-start | bytes 12292
  19.1 23.9 %copy-start.7 = (pred[4096]{0:T(1024)(128)(4,1)S(1)}, pred[4096]{0:T(1024)(128)(4,1)}, u32[]{:S(2)}) copy-start(pred[4096]{0:T(1024)(128)(4,1)} %constant.245) | copy-start | bytes 12292
  23.3 69.5 %all-to-all-start = ((bf16[128,32,256]{2,0,1:T(8,128)(2,1)}), bf16[128,32,256]{2,0,1:T(8,128)(2,1)S(1)}, u32[]{:S(2)}, u32[]{:S(2)}) async-start(bf16[128,32,256]{2,0,1:T(8,128)(2,1)} %copy.23), calls=%async_computation | async-start | bytes 4194304 | tf_op jit(solution)/shard_map/all_to_all | solution.py:128
  39.3 781.2 %reduce-scatter.4.cloned.1.call-start = ((), (), s32[]{:S(2)}) async-start(), calls=%async_computation.4 | async-start | bytes 2162688
  538.7 14.2 %copy-start.4 = (bf16[256,4096]{1,0:T(8,128)(2,1)S(1)}, bf16[256,4096]{1,0:T(8,128)(2,1)}, u32[]{:S(2)}) copy-start(bf16[256,4096]{1,0:T(8,128)(2,1)} %all-gather.4.cloned.1.call-done) | copy-start | bytes 6291460
  548.1 27.6 %collective-permute-start = (bf16[4096,256]{1,0:T(8,128)(2,1)}, bf16[4096,256]{1,0:T(8,128)(2,1)S(1)}, u32[]{:S(2)}, u32[]{:S(2)}) collective-permute-start(bf16[4096,256]{1,0:T(8,128)(2,1)} %scatter_custom_fusion), channel_id=1, source_target_pairs={{0,1},{1,2},{2,3},{3,4},{4,5},{5,6},{6,7},{7,8},{8,9},{9,10},{10,1... | collective-permute-start | bytes 6291464 | tf_op jit(solution)/shard_map/ppermute | solution.py:27
  575.6 1.8 copy-start.9
  577.4 5.8 copy-start.2
  577.4 5.8 copy-start.3
Sparse Core Ops, SparseCore 0:
  10.4 130.9 all-gather.3
  144.6 380.9 all-gather.5
  594.7 225.7 reduce-scatter.3
